TPU v7x, 32 devices: a whole 2x2x4 slice. The times are simulated.
32 devices in a mesh: grp: 2 (over y), frame: 4 (over x, core), coil: 4 (over z).
Axes of the slice: x: 2, y: 2, z: 4, core: 2. Of those that a mesh axis runs over, the one named last changes fastest.
Arguments:
- images: bfloat16 [8, 2, 384, 384], P(('grp', 'frame')), parts along dimension 0, may hold values from -6 to 6
- coil_maps: bfloat16 [8, 2, 384, 384], P(('grp', 'coil')), parts along dimension 0, may hold values from -3 to 3
- kspace_data: float32 [8, 4, 2, 6, 128], P(('grp', 'frame'), 'coil'), parts along dimension 0, may hold values from -6 to 6
- spoke_angle: int32 [8, 6], P(('grp', 'frame')), parts along dimension 0, may hold values from 0 to 15
- band_row: int32 [8, 6], P(('grp', 'frame')), parts along dimension 0, may hold values from 0 to 256
- band_col: int32 [8, 6], P(('grp', 'frame')), parts along dimension 0, may hold values from 0 to 256
- kernel_rows: bfloat16 [16, 128, 128], replicated, may hold values from -0.5 to 0.5
- kernel_cols: bfloat16 [16, 128, 128], replicated, may hold values from -0.5 to 0.5
Outputs:
- updated: float32 [8, 2, 384, 384], P(('grp', 'frame')), parts along dimension 0
There are 2 independent parts, one for each index of `grp`. A program takes and returns all parts, laid end to end along the dimension named above; an argument that names none is the same for every part. Nothing has to cross between parts.
All inputs are finite; a program needn't handle non-finite values.
Results may differ from a plain program's by a relative error of at most 0.0014.
Values may be sent and summed in bfloat16 or wider, within the bound.
No kernel may reach another device: no remote copies, remote signals or barrier semaphores. Data moves between devices by JAX's collectives and lax.ppermute only.
A program may use at most 64 MiB of HBM per device.

v0:
```python
import math
import jax
import jax.numpy as jnp
from jax import lax
from jax.sharding import PartitionSpec as P

SMOOTHING = 0.05
STEP_SIZE = 1.0
TV_WEIGHT = 0.2


def padded(cells, sides, width):
    for axis, dim in sides:
        count = lax.axis_size(axis)
        ends = count - 1
        head = lax.slice_in_dim(cells, 0, width, axis=dim)
        tail = lax.slice_in_dim(cells, cells.shape[dim] - width, cells.shape[dim], axis=dim)
        cells = jnp.concatenate(
            [
                lax.ppermute(tail, axis, [(i, (i + 1) % count) for i in range(ends)]),
                cells,
                lax.ppermute(head, axis, [((i + 1) % count, i) for i in range(ends)]),
            ],
            axis=dim,
        )
    return cells


def transform_table(extent):
    indices = jnp.arange(extent, dtype=jnp.int32)
    phases = indices[:, None] * indices[None, :] % extent
    angle_values = 2.0 * math.pi / extent * phases.astype(jnp.float32)
    scaling = 1.0 / math.sqrt(extent)
    return jnp.stack([jnp.cos(angle_values) * scaling, jnp.sin(angle_values) * scaling]).astype(
        jnp.bfloat16
    )


def combine_parts(products, direction):
    real_part = products[0, 0] + direction * products[1, 1]
    imaginary = products[0, 1] - direction * products[1, 0]
    return jnp.stack([real_part, imaginary])


def left_apply(transform, planes, direction):
    products = jnp.einsum("aij,bjk->abik", transform, planes, preferred_element_type=jnp.float32)
    return combine_parts(products, direction)


def right_apply(transform, planes, direction):
    products = jnp.einsum("bij,ajk->abik", planes, transform, preferred_element_type=jnp.float32)
    return combine_parts(products, direction)


def selector(first_index, extent, patch_side, kind):
    positions = jnp.arange(extent, dtype=jnp.int32)
    offsets = jnp.arange(patch_side, dtype=jnp.int32)
    wanted = first_index[:, None, None] + offsets[None, None, :]
    return (positions[None, :, None] == wanted).astype(kind)


def cut_windows(kspace, row_first, col_first, patch_side):
    extent = kspace.shape[-1]
    row_select = selector(row_first, extent, patch_side, jnp.bfloat16)
    col_select = selector(col_first, extent, patch_side, jnp.bfloat16)
    picked_rows = jnp.einsum(
        "tir,bik->tbrk", row_select, kspace, preferred_element_type=jnp.float32
    ).astype(jnp.bfloat16)
    return jnp.einsum(
        "tbrk,tkq->tbrq", picked_rows, col_select, preferred_element_type=jnp.float32
    ).astype(jnp.bfloat16)


def add_windows(windows, row_first, col_first, extent):
    patch_side = windows.shape[-1]
    row_select = selector(row_first, extent, patch_side, jnp.float32)
    col_select = selector(col_first, extent, patch_side, jnp.float32)
    placed = jnp.einsum("tbrq,tkq->tbrk", windows, col_select, precision=lax.Precision.HIGHEST)
    return jnp.einsum("tir,tbrk->bik", row_select, placed, precision=lax.Precision.HIGHEST)


def coil_gradient(
    transform,
    frame_image,
    coil_map,
    measured,
    angle_ids,
    row_first,
    col_first,
    kernel_rows,
    kernel_cols,
):
    extent = frame_image.shape[-1]
    patch_side = kernel_cols.shape[-1]
    map_planes = coil_map.astype(jnp.float32)
    image_planes = frame_image.astype(jnp.float32)
    coil_image = jnp.stack(
        [
            map_planes[0] * image_planes[0] - map_planes[1] * image_planes[1],
            map_planes[0] * image_planes[1] + map_planes[1] * image_planes[0],
        ]
    ).astype(jnp.bfloat16)
    half_done = left_apply(transform, coil_image, 1.0).astype(jnp.bfloat16)
    kspace = right_apply(transform, half_done, 1.0).astype(jnp.bfloat16)
    patches = cut_windows(kspace, row_first, col_first, patch_side)
    row_weights = kernel_rows[angle_ids]
    col_weights = kernel_cols[angle_ids]
    contracted = jnp.einsum(
        "tprq,tjq->ptrj", patches, col_weights, preferred_element_type=jnp.float32
    )
    predicted = jnp.sum(contracted * row_weights[None], axis=2)
    residual = predicted - measured
    spread = (row_weights[None] * residual[:, :, None, :]).astype(jnp.bfloat16)
    spread_back = jnp.einsum(
        "ptrj,tjq->tprq", spread, col_weights, preferred_element_type=jnp.float32
    )
    gridded = add_windows(spread_back, row_first, col_first, extent)
    gridded = gridded.astype(jnp.bfloat16)
    half_back = left_apply(transform, gridded, -1.0).astype(jnp.bfloat16)
    coil_back = right_apply(transform, half_back, -1.0)
    return jnp.stack(
        [
            map_planes[0] * coil_back[0] + map_planes[1] * coil_back[1],
            map_planes[0] * coil_back[1] - map_planes[1] * coil_back[0],
        ]
    )


def apply_update(own_rows, extended, data_grad, first_frame, frame_total):
    widened = extended.astype(jnp.float32)
    change = widened[1:] - widened[:-1]
    position = first_frame - 1 + jnp.arange(change.shape[0], dtype=jnp.int32)
    inside = ((position >= 0) & (position <= frame_total - 2)).astype(jnp.float32)
    normed = inside[:, None, None, None] * (
        change / jnp.sqrt(jnp.sum(change * change, axis=1, keepdims=True) + SMOOTHING)
    )
    tv_grad = normed[:-1] - normed[1:]
    return own_rows.astype(jnp.float32) - STEP_SIZE * (data_grad + TV_WEIGHT * tv_grad)


def local(
    images, coil_maps, kspace_data, spoke_angle, band_row, band_col, kernel_rows, kernel_cols
):
    frame_count = images.shape[0]
    transform = transform_table(images.shape[-1])
    running = coil_gradient(
        transform,
        images[0],
        coil_maps[0],
        kspace_data[0, 0],
        spoke_angle[0],
        band_row[0],
        band_col[0],
        kernel_rows,
        kernel_cols,
    )
    gradients = [running]
    data_terms = jnp.stack(gradients)
    first_frame = lax.axis_index("frame") * frame_count
    frame_total = lax.axis_size("frame") * frame_count
    extended = padded(images, (("frame", 0),), 1)
    data_grad = lax.psum(data_terms.astype(jnp.bfloat16), "coil").astype(jnp.float32)
    return apply_update(images, extended, data_grad, first_frame, frame_total)


def solution(mesh):
    in_specs = (
        P(("grp", "frame"), None, None, None),
        P(("grp", "coil"), None, None, None),
        P(("grp", "frame"), "coil", None, None, None),
        P(("grp", "frame"), None),
        P(("grp", "frame"), None),
        P(("grp", "frame"), None),
        P(),
        P(),
    )
    out_specs = P(("grp", "frame"), None, None, None)
    return jax.shard_map(local, mesh=mesh, in_specs=in_specs, out_specs=out_specs, check_vma=False)
```

profile of v0, /device:TPU:0, one launch (start us, length us, event | category | flops | bytes accessed | tf_op | source)
XLA Modules:
  0.0 91.9 jit_solution(15855914148542029132)
XLA Ops:
  6.5 0.0 copy-start
  6.5 0.0 all-reduce.2.cloned.1.call-start
  6.5 1.4 %copy.23 = bf16[1,2,384,384]{2,3,1,0:T(8,128)(2,1)S(1)} copy(bf16[1,2,384,384]{3,2,1,0:T(8,128)(2,1)} %param.8) | data formatting | bytes 1179648 | tf_op args[0]
  8.0 0.0 copy-start.2
  8.0 1.4 %collective-permute-start.1 = (bf16[1,2,384,384]{2,3,1,0:T(8,128)(2,1)S(1)}, bf16[1,2,384,384]{2,3,1,0:T(8,128)(2,1)}, u32[]{:S(2)}, u32[]{:S(2)}) collective-permute-start(bf16[1,2,384,384]{2,3,1,0:T(8,128)(2,1)S(1)} %copy.23), channel_id=1, source_target_pairs={{4,0},{8,4},{12,8},{5,1},{9,5},{13,9},{6,2},{10,6},{14,10},{7,3},{... | collective-permute-start | bytes 1769480 | tf_op jit(solution)/shard_map/ppermute | solution.py:22
  9.4 3.9 %collective-permute-start = (bf16[1,2,384,384]{2,3,1,0:T(8,128)(2,1)S(1)}, bf16[1,2,384,384]{2,3,1,0:T(8,128)(2,1)}, u32[]{:S(2)}, u32[]{:S(2)}) collective-permute-start(bf16[1,2,384,384]{2,3,1,0:T(8,128)(2,1)S(1)} %copy.23), channel_id=1, source_target_pairs={{0,4},{4,8},{8,12},{1,5},{5,9},{9,13},{2,6},{6,10},{10,14},{3,7},{... | collective-permute-start | bytes 1769480 | tf_op jit(solution)/shard_map/ppermute | solution.py:20
  13.3 1.1 %convert_element_type.83 = f32[1,2,384,384]{2,3,1,0:T(8,128)} convert(bf16[1,2,384,384]{2,3,1,0:T(8,128)(2,1)S(1)} %copy.23) | non-fusion elementwise | flops 294912 | bytes 1769472 | tf_op jit(solution)/shard_map/convert_element_type | solution.py:138
  14.4 2.6 %multiply_convert_fusion.1 = (bf16[1,384,384]{2,1,0:T(8,128)(2,1)S(1)}, bf16[1,384,384]{2,1,0:T(8,128)(2,1)S(1)}) fusion(), kind=kLoop, calls=%fused_computation.82 | loop fusion | flops 1916928 | bytes 589824 | tf_op jit(solution)/shard_map/convert.19
  17.0 0.0 copy-done.2
  17.0 0.3 copy.24
  17.3 0.0 copy-start.1
  17.3 0.1 convert_element_type.84
  17.4 1.2 %copy-done.1 = f32[1,2,384,384]{2,3,1,0:T(8,128)S(1)} copy-done((f32[1,2,384,384]{2,3,1,0:T(8,128)S(1)}, f32[1,2,384,384]{2,3,1,0:T(8,128)}, u32[]{:S(2)}) %copy-start.1) | copy-done | bytes 1179672
  18.6 0.2 fusion.53
  18.7 0.8 convolution_bitcast_fusion.3
  19.5 0.0 copy-start.6
  19.6 0.1 fusion.56
  19.6 0.1 fusion.55
  19.7 0.5 copy-done.6
  20.2 0.8 convolution_bitcast_fusion.2
  21.0 0.0 copy-start.4
  21.0 0.1 fusion.57
  21.2 0.5 copy-done.4
  21.7 0.1 iota_add_fusion.1
  21.8 0.8 fusion.11
  22.6 0.0 copy-start.5
  22.6 2.0 %copy.70 = bf16[2,384,6,128]{3,2,1,0:T(8,128)(2,1)} copy(bf16[2,384,6,128]{3,1,2,0:T(8,128)(2,1)S(1)} %fusion.11) | data formatting | bytes 2359296 | tf_op jit(solution)/shard_map/tir,bik->tbrk/dot_general | solution.py:66
  24.6 0.0 copy-done.5
  24.6 0.1 iota_add_fusion
  24.7 0.0 copy-done
  24.7 0.6 gather_fusion.1
  25.3 1.6 %gather_fusion = bf16[6,128,128]{2,1,0:T(8,128)(2,1)S(1)} fusion(bf16[16,128,128]{2,1,0:T(8,128)(2,1)} %param.14, s32[1024]{0:T(1024)S(1)} %pad_clamp_fusion), kind=kCustom, calls=%fused_computation | custom fusion | bytes 393240 | tf_op jit(solution)/shard_map/gather | solution.py:106
  26.9 0.0 copy-start.3
  26.9 2.0 %convolution_convert_fusion = bf16[6,2,128,128]{3,2,1,0:T(8,128)(2,1)S(1)} fusion(bf16[6,2,128,384]{2,0,3,1:T(8,128)(2,1)} %bitcast.119, s32[6,128]{1,0:T(8,128)S(1)} %iota_add_fusion), kind=kOutput, calls=%fused_computation.17 | convolution fusion | flops 151486464 | bytes 1575936 | tf_op jit(solution)/shard_map/tbrk,tkq->tbrq/dot_general | solution.py:69
  29.0 0.3 fusion.4
  29.3 0.0 copy-done.3
  29.3 0.3 fusion.50
  29.6 1.1 %fusion.15 = f32[6,2,128,384]{3,2,1,0:T(8,128)S(1)} fusion(f32[6,2,128,128]{3,2,1,0:T(8,128)S(1)} %fusion.50, s32[6,128]{1,0:T(8,128)S(1)} %iota_add_fusion), kind=kOutput, calls=%fused_computation.31 | convolution fusion | flops 906264576 | bytes 3148800 | tf_op jit(solution)/shard_map/tbrq,tkq->tbrk/dot_general | solution.py:78
  30.7 3.9 %fusion.3 = bf16[2,384,384,1]{1,2,0,3:T(8,128)(2,1)S(1)} fusion(f32[6,2,128,384]{3,2,1,0:T(8,128)S(1)} %fusion.15, s32[6,128]{1,0:T(8,128)S(1)} %iota_add_fusion.1), kind=kOutput, calls=%fused_computation.16 | convolution fusion | flops 2718498816 | bytes 2952192 | tf_op jit(solution)/shard_map/tir,tbrk->bik/dot_general | solution.py:79
  34.6 0.8 convolution_bitcast_fusion.1
  35.4 0.1 fusion.59
  35.6 0.8 convolution_bitcast_fusion
  36.4 0.3 add_convert_fusion
  36.6 0.9 pad_maximum_fusion.1
  37.5 0.0 all-reduce.2.cloned.1.call-update
  37.6 0.0 collective-permute-done.1
  37.6 0.0 collective-permute-done
  37.6 1.5 %maximum_convert_fusion = f32[3,2,384,384]{2,3,1,0:T(8,128)S(1)} fusion(bf16[1,2,384,384]{2,3,1,0:T(8,128)(2,1)} %collective-permute-done.1, bf16[1,2,384,384]{2,3,1,0:T(8,128)(2,1)S(1)} %copy.23, bf16[1,2,384,384]{2,3,1,0:T(8,128)(2,1)} %collective-permute-done), kind=kLoop, calls=%fused_computation.6 | loop fusion | flops 2654208 | bytes 5308416 | tf_op jit(solution)/shard_map/convert_element_type | solution.py:130
  39.1 0.3 multiply_reduce_fusion
  39.4 0.3 add_sqrt_fusion
  39.7 0.3 divide_multiply_fusion
  40.0 40.0 %all-reduce.2.cloned.1.call-done = bf16[1,2,384,384]{2,3,1,0:T(8,128)(2,1)} async-done(((bf16[1,2,384,384]{2,3,1,0:T(8,128)(2,1)}), bf16[1,2,384,384]{2,3,1,0:T(8,128)(2,1)}) %all-reduce.2.cloned.1.call-update) | async-done | bytes 589840 | tf_op jit(solution)/shard_map/psum | solution.py:162
  80.0 2.3 %fusion.7 = f32[1,2,384,384]{2,3,1,0:T(8,128)} fusion(f32[2,2,384,384]{2,3,1,0:T(8,128)S(1)} %divide_multiply_fusion, bf16[1,2,384,384]{2,3,1,0:T(8,128)(2,1)} %all-reduce.2.cloned.1.call-done, bf16[1,2,384,384]{2,3,1,0:T(8,128)(2,1)S(1)} %copy.23), kind=kLoop, calls=%fused_computation.22 | loop fusion | flops 1769472 | bytes 4718592 | tf_op jit(solution)/shard_map/sub | solution.py:138
  82.4 2.7 %copy.36 = f32[1,2,384,384]{3,2,1,0:T(8,128)} copy(f32[1,2,384,384]{2,3,1,0:T(8,128)} %fusion.7) | data formatting | bytes 2359296 | tf_op jit(solution)/shard_map/sub | solution.py:138
  (5 shorter events, 0.1 us)
Async XLA Ops:
  6.5 18.1 %copy-start = (bf16[16,128,128]{2,1,0:T(8,128)(2,1)S(1)}, bf16[16,128,128]{2,1,0:T(8,128)(2,1)}, u32[]{:S(2)}) copy-start(bf16[16,128,128]{2,1,0:T(8,128)(2,1)} %param.15) | copy-start | bytes 1572868
  6.5 73.5 %all-reduce.2.cloned.1.call-start = ((), (), s32[]{:S(2)}) async-start(), calls=%async_computation | async-start | bytes 1179648 | tf_op jit(solution)/shard_map/psum | solution.py:162
  8.0 9.0 %copy-start.2 = (bf16[1,2,384,384]{3,2,1,0:T(8,128)(2,1)S(1)}, bf16[1,2,384,384]{3,2,1,0:T(8,128)(2,1)}, u32[]{:S(2)}) copy-start(bf16[1,2,384,384]{3,2,1,0:T(8,128)(2,1)} %param.9) | copy-start | bytes 1769476
  8.0 29.6 %collective-permute-start.1 = (bf16[1,2,384,384]{2,3,1,0:T(8,128)(2,1)S(1)}, bf16[1,2,384,384]{2,3,1,0:T(8,128)(2,1)}, u32[]{:S(2)}, u32[]{:S(2)}) collective-permute-start(bf16[1,2,384,384]{2,3,1,0:T(8,128)(2,1)S(1)} %copy.23), channel_id=1, source_target_pairs={{4,0},{8,4},{12,8},{5,1},{9,5},{13,9},{6,2},{10,6},{14,10},{7,3},{... | collective-permute-start | bytes 1769480 | tf_op jit(solution)/shard_map/ppermute | solution.py:22
  9.4 28.2 %collective-permute-start = (bf16[1,2,384,384]{2,3,1,0:T(8,128)(2,1)S(1)}, bf16[1,2,384,384]{2,3,1,0:T(8,128)(2,1)}, u32[]{:S(2)}, u32[]{:S(2)}) collective-permute-start(bf16[1,2,384,384]{2,3,1,0:T(8,128)(2,1)S(1)} %copy.23), channel_id=1, source_target_pairs={{0,4},{4,8},{8,12},{1,5},{5,9},{9,13},{2,6},{6,10},{10,14},{3,7},{... | collective-permute-start | bytes 1769480 | tf_op jit(solution)/shard_map/ppermute | solution.py:20
  17.3 1.3 %copy-start.1 = (f32[1,2,384,384]{2,3,1,0:T(8,128)S(1)}, f32[1,2,384,384]{2,3,1,0:T(8,128)}, u32[]{:S(2)}) copy-start(f32[1,2,384,384]{2,3,1,0:T(8,128)} %convert_element_type.83) | copy-start | bytes 3538948
  19.5 0.7 copy-start.6
  21.0 0.7 copy-start.4
  22.6 2.0 %copy-start.5 = (s32[1,6]{1,0:T(1,128)S(1)}, s32[1,6]{1,0:T(1,128)}, u32[]{:S(2)}) copy-start(s32[1,6]{1,0:T(1,128)} %param.13) | copy-start | bytes 76
  26.9 2.4 %copy-start.3 = (f32[1,1,2,6,128]{4,2,3,1,0:T(2,128)S(1)}, f32[1,1,2,6,128]{4,2,3,1,0:T(2,128)}, u32[]{:S(2)}) copy-start(f32[1,1,2,6,128]{4,2,3,1,0:T(2,128)} %param.10) | copy-start | bytes 18436
Sparse Core Ops, SparseCore 0:
  37.7 42.3 all-reduce.1
where the time goes:
time: 92.3 us; the launch traced here: 91.9 us
  waiting for transfers between devices  40 us (43%)
  between operations  13.7 us (15%)
  matrix products  11.7 us (13%)
  local copies, waits for them, and re-layouts  10.8 us (12%)
  other arithmetic  10.4 us (11%)
  starting transfers between devices  5.29 us (6%)
    psum x1, waiting for transfers between devices, local(): lax.psum(data_terms.astype(jnp.bfloat16), 'coil').astype(jnp.float32)  40 us
    unnamed x16, local copies, waits for them, and re-layouts  3.99 us
    dot_general x1, matrix products, add_windows(): jnp.einsum('tir,tbrk->bik', row_select, placed, precision=lax.Precision.H...  3.92 us
    ppermute x1, starting transfers between devices, padded(): lax.ppermute(tail, axis, [(i, (i + 1) % count) for i in range(ends)])  3.86 us
    another operation x2, other arithmetic  2.84 us
    sub x1, local copies, waits for them, and re-layouts, apply_update(): own_rows.astype(jnp.float32) - STEP_SIZE * (data_grad + TV_WEIGHT * tv_grad)  2.65 us
    sub x1, other arithmetic, apply_update(): own_rows.astype(jnp.float32) - STEP_SIZE * (data_grad + TV_WEIGHT * tv_grad)  2.33 us
    dot_general x1, matrix products, cut_windows(): jnp.einsum('tbrk,tkq->tbrq', picked_rows, col_select, preferred_element_t...  2.05 us
  transfers between devices with their start and end apart: 3, of which 1 were waited for; matrix products, arithmetic and copies ran while one was open for 26% of the time, Pallas kernels for 0%

commit v1 on v0

--- a/solution.py
+++ b/solution.py
@@ -159,7 +159,9 @@
     first_frame = lax.axis_index("frame") * frame_count
     frame_total = lax.axis_size("frame") * frame_count
     extended = padded(images, (("frame", 0),), 1)
-    data_grad = lax.psum(data_terms.astype(jnp.bfloat16), "coil").astype(jnp.float32)
+    data_grad = jnp.sum(lax.all_gather(data_terms.astype(jnp.bfloat16), "coil"), axis=0).astype(
+        jnp.float32
+    )
     return apply_update(images, extended, data_grad, first_frame, frame_total)
 
 

time: 92.3 us -> 96.6 us (1.047)
  waiting for transfers between devices: 40 us -> 47.1 us
  matrix products: 11.7 us -> 9.44 us
    all_gather x0 -> x1, waiting for transfers between devices: none -> 45.7 us  [local(): lax.all_gather(data_terms.astype(jnp.bfloat16), 'coil')]
    psum x1 -> x0, waiting for transfers between devices: 40 us -> none  [local(): lax.psum(data_terms.astype(jnp.bfloat16), 'coil').astype(jnp.float32)]
    reduce_sum x0 -> x1, other arithmetic: none -> 2.99 us  [local(): jnp.sum(lax.all_gather(data_terms.astype(jnp.bfloat16), 'coil'), axis=0)]
    reduce_sum x0 -> x1, local copies, waits for them, and re-layouts: none -> 2.14 us  [local(): jnp.sum(lax.all_gather(data_terms.astype(jnp.bfloat16), 'coil'), axis=0)]
    dot_general x1 -> x0, local copies, waits for them, and re-layouts: 1.98 us -> none  [cut_windows(): jnp.einsum('tir,bik->tbrk', row_select, kspace, preferred_element_type=jn...]
    dot_general x1, matrix products: 3.92 us -> 2.04 us  [add_windows(): jnp.einsum('tir,tbrk->bik', row_select, placed, precision=lax.Precision.H...]
    unnamed x16 -> x14, local copies, waits for them, and re-layouts: 3.99 us -> 2.23 us
    dot_general x1, matrix products: 2.05 us -> 0.62 us  [cut_windows(): jnp.einsum('tbrk,tkq->tbrq', picked_rows, col_select, preferred_element_t...]
  transfers between devices with their start and end apart: 3 -> 3, of which waited for: 1 -> 2; matrix products, arithmetic and copies ran while one was open for 26% -> 1% of each run, Pallas kernels for 0% -> 0%
where the time goes in v1:
time: 96.6 us; the launch traced here: 96.2 us
  waiting for transfers between devices  47.1 us (49%)
  between operations  13.7 us (14%)
  other arithmetic  11.1 us (11%)
  local copies, waits for them, and re-layouts  10.3 us (11%)
  matrix products  9.44 us (10%)
  starting transfers between devices  4.54 us (5%)
    all_gather x1, waiting for transfers between devices, local(): lax.all_gather(data_terms.astype(jnp.bfloat16), 'coil')  45.7 us
    ppermute x1, starting transfers between devices, padded(): lax.ppermute(tail, axis, [(i, (i + 1) % count) for i in range(ends)])  3.25 us
    reduce_sum x1, other arithmetic, local(): jnp.sum(lax.all_gather(data_terms.astype(jnp.bfloat16), 'coil'), axis=0)  2.99 us
    sub x1, local copies, waits for them, and re-layouts, apply_update(): own_rows.astype(jnp.float32) - STEP_SIZE * (data_grad + TV_WEIGHT * tv_grad)  2.65 us
    another operation x1, other arithmetic  2.58 us
    sub x1, other arithmetic, apply_update(): own_rows.astype(jnp.float32) - STEP_SIZE * (data_grad + TV_WEIGHT * tv_grad)  2.31 us
    unnamed x14, local copies, waits for them, and re-layouts  2.23 us
    reduce_sum x1, local copies, waits for them, and re-layouts, local(): jnp.sum(lax.all_gather(data_terms.astype(jnp.bfloat16), 'coil'), axis=0)  2.14 us
  transfers between devices with their start and end apart: 3, of which 2 were waited for; matrix products, arithmetic and copies ran while one was open for 1% of the time, Pallas kernels for 0%

profile of v1, /device:TPU:0, one launch (start us, length us, event | category | flops | bytes accessed | tf_op | source)
XLA Modules:
  0.0 96.2 jit_solution(14747610000078617978)
XLA Ops:
  6.5 0.0 copy-start
  6.5 0.0 copy-start.1
  6.5 0.0 all-gather.2.cloned.1.call-start
  6.5 2.6 %multiply_convert_fusion.1 = (bf16[1,384,384]{2,1,0:T(8,128)(2,1)S(1)}, bf16[1,384,384]{2,1,0:T(8,128)(2,1)S(1)}) fusion(), kind=kLoop, calls=%fused_computation.81 | loop fusion | flops 1916928 | bytes 589824 | tf_op jit(solution)/shard_map/convert.23
  9.1 1.4 %copy.58 = bf16[1,2,384,384]{2,3,1,0:T(8,128)(2,1)S(1)} copy(bf16[1,2,384,384]{3,2,1,0:T(8,128)(2,1)} %param.8) | data formatting | bytes 1179648 | tf_op args[0]
  10.5 0.0 copy-done.1
  10.5 0.3 copy.59
  10.8 0.1 convert_element_type.98
  10.9 0.1 convert_element_type.97
  11.0 0.2 fusion.52
  11.2 0.8 convolution_bitcast_fusion.3
  12.0 0.0 copy-start.5
  12.0 0.1 fusion.57
  12.1 0.1 fusion.56
  12.1 0.5 copy-done.5
  12.7 0.8 convolution_bitcast_fusion.2
  13.5 0.0 copy-start.3
  13.5 0.0 copy-start.4
  13.5 0.9 fusion.58
  14.4 0.0 copy-done.3
  14.4 0.1 iota_add_fusion.1
  14.5 0.0 copy-done.4
  14.5 0.1 iota_add_fusion
  14.6 0.0 copy-done
  14.6 0.6 gather_fusion.1
  15.2 1.6 %gather_fusion = bf16[6,128,128]{2,1,0:T(8,128)(2,1)S(1)} fusion(bf16[16,128,128]{2,1,0:T(8,128)(2,1)} %param.14, s32[1024]{0:T(1024)S(1)} %pad_clamp_fusion), kind=kCustom, calls=%fused_computation | custom fusion | bytes 393240 | tf_op jit(solution)/shard_map/gather | solution.py:106
  16.8 1.9 %fusion = bf16[6,2,128,384]{2,3,0,1:T(8,128)(2,1)S(1)} fusion(bf16[1,384,384]{1,2,0:T(8,128)(2,1)} %get-tuple-element.10, bf16[1,384,384]{1,2,0:T(8,128)(2,1)} %get-tuple-element.9, s32[6,128]{1,0:T(8,128)S(1)} %iota_add_fusion.1), kind=kOutput, calls=%fused_computation.11 | convolution fusion | flops 455049216 | bytes 1772544 | tf_op jit(solution)/shard_map/tir,bik->tbrk/dot_general | solution.py:66
  18.7 0.0 copy-start.2
  18.7 0.6 convolution_convert_fusion.1
  19.3 0.3 fusion.4
  19.6 0.0 copy-done.2
  19.7 0.3 fusion.49
  19.9 1.2 %fusion.14 = f32[6,2,128,384]{2,3,1,0:T(8,128)S(1)} fusion(f32[6,2,128,128]{3,2,1,0:T(8,128)S(1)} %fusion.49, s32[6,128]{1,0:T(8,128)S(1)} %iota_add_fusion), kind=kOutput, calls=%fused_computation.30 | convolution fusion | flops 906264576 | bytes 3148800 | tf_op jit(solution)/shard_map/tbrq,tkq->tbrk/dot_general | solution.py:78
  21.1 2.0 %fusion.3 = bf16[2,384,384,1]{1,2,0,3:T(8,128)(2,1)S(1)} fusion(f32[6,2,128,384]{2,3,1,0:T(8,128)S(1)} %fusion.14, s32[6,128]{1,0:T(8,128)S(1)} %iota_add_fusion.1), kind=kOutput, calls=%fused_computation.16 | convolution fusion | flops 2718498816 | bytes 2952192 | tf_op jit(solution)/shard_map/tir,tbrk->bik/dot_general | solution.py:79
  23.1 0.8 convolution_bitcast_fusion.1
  23.9 0.1 fusion.60
  24.1 0.8 convolution_bitcast_fusion
  24.9 0.3 fusion.54
  25.2 0.1 pad_maximum_fusion.1
  25.2 1.1 %copy.72 = bf16[1,1,2,384,384]{4,3,2,1,0:T(8,128)(2,1)} copy(bf16[1,1,2,384,384]{3,4,2,1,0:T(8,128)(2,1)S(1)} %pad_maximum_fusion.1) | data formatting | bytes 1179648 | tf_op jit(solution)/shard_map/stack | solution.py:121
  26.3 0.0 all-gather.2.cloned.1.call-update
  26.3 1.3 %collective-permute-start.1 = (bf16[1,2,384,384]{2,3,1,0:T(8,128)(2,1)S(1)}, bf16[1,2,384,384]{2,3,1,0:T(8,128)(2,1)S(1)}, u32[]{:S(2)}, u32[]{:S(2)}) collective-permute-start(bf16[1,2,384,384]{2,3,1,0:T(8,128)(2,1)S(1)} %copy.58), channel_id=1, source_target_pairs={{4,0},{8,4},{12,8},{5,1},{9,5},{13,9},{6,2},{10,6},{14,10},{7,3},{... | collective-permute-start | bytes 1769480 | tf_op jit(solution)/shard_map/ppermute | solution.py:22
  27.6 3.2 %collective-permute-start = (bf16[1,2,384,384]{2,3,1,0:T(8,128)(2,1)S(1)}, bf16[1,2,384,384]{2,3,1,0:T(8,128)(2,1)S(1)}, u32[]{:S(2)}, u32[]{:S(2)}) collective-permute-start(bf16[1,2,384,384]{2,3,1,0:T(8,128)(2,1)S(1)} %copy.58), channel_id=1, source_target_pairs={{0,4},{4,8},{8,12},{1,5},{5,9},{9,13},{2,6},{6,10},{10,14},{3,7},{... | collective-permute-start | bytes 1769480 | tf_op jit(solution)/shard_map/ppermute | solution.py:20
  30.9 0.0 collective-permute-done.1
  30.9 1.4 %collective-permute-done = bf16[1,2,384,384]{2,3,1,0:T(8,128)(2,1)S(1)} collective-permute-done((bf16[1,2,384,384]{2,3,1,0:T(8,128)(2,1)S(1)}, bf16[1,2,384,384]{2,3,1,0:T(8,128)(2,1)S(1)}, u32[]{:S(2)}, u32[]{:S(2)}) %collective-permute-start) | collective-permute-done | bytes 589856 | tf_op jit(solution)/shard_map/ppermute | solution.py:20
  32.3 0.3 maximum_convert_fusion
  32.6 0.3 multiply_reduce_fusion
  32.8 0.3 add_sqrt_fusion
  33.1 0.3 divide_multiply_fusion
  33.5 45.7 %all-gather.2.cloned.1.call-done = bf16[4,1,2,384,384]{4,3,2,1,0:T(8,128)(2,1)} async-done(((bf16[1,1,2,384,384]{4,3,2,1,0:T(8,128)(2,1)}), bf16[4,1,2,384,384]{4,3,2,1,0:T(8,128)(2,1)}) %all-gather.2.cloned.1.call-update) | async-done | bytes 2359312 | tf_op jit(solution)/shard_map/all_gather | solution.py:162
  79.2 3.0 %reduce_sum.31 = bf16[2,384,384]{2,1,0:T(8,128)(2,1)} reduce(bf16[4,1,2,384,384]{4,3,2,1,0:T(8,128)(2,1)} %all-gather.2.cloned.1.call-done, bf16[]{:T(256)} %constant.33.clone.1), dimensions={0,1}, to_apply=%region_1.2 | reduce | flops 884736 | bytes 2949122 | tf_op jit(solution)/shard_map/reduce_sum | solution.py:162
  82.2 2.1 %copy.73 = bf16[2,384,384]{1,2,0:T(8,128)(2,1)} copy(bf16[2,384,384]{2,1,0:T(8,128)(2,1)} %reduce_sum.31) | data formatting | bytes 1179648 | tf_op jit(solution)/shard_map/reduce_sum | solution.py:162
  84.3 2.3 %fusion.7 = f32[1,2,384,384]{2,3,1,0:T(8,128)} fusion(f32[2,2,384,384]{2,3,1,0:T(8,128)S(1)} %divide_multiply_fusion, bf16[2,384,384]{1,2,0:T(8,128)(2,1)} %copy.73, bf16[1,2,384,384]{2,3,1,0:T(8,128)(2,1)S(1)} %copy.58), kind=kLoop, calls=%fused_computation.22 | loop fusion | flops 1769472 | bytes 4718592 | tf_op jit(solution)/shard_map/sub | solution.py:138
  86.7 2.7 %copy.77 = f32[1,2,384,384]{3,2,1,0:T(8,128)} copy(f32[1,2,384,384]{2,3,1,0:T(8,128)} %fusion.7) | data formatting | bytes 2359296 | tf_op jit(solution)/shard_map/sub | solution.py:138
  (5 shorter events, 0.1 us)
Async XLA Ops:
  6.5 8.0 %copy-start = (bf16[16,128,128]{2,1,0:T(8,128)(2,1)S(1)}, bf16[16,128,128]{2,1,0:T(8,128)(2,1)}, u32[]{:S(2)}) copy-start(bf16[16,128,128]{2,1,0:T(8,128)(2,1)} %param.15) | copy-start | bytes 1572868
  6.5 4.0 %copy-start.1 = (bf16[1,2,384,384]{3,2,1,0:T(8,128)(2,1)S(1)}, bf16[1,2,384,384]{3,2,1,0:T(8,128)(2,1)}, u32[]{:S(2)}) copy-start(bf16[1,2,384,384]{3,2,1,0:T(8,128)(2,1)} %param.9) | copy-start | bytes 1769476
  6.5 72.7 %all-gather.2.cloned.1.call-start = ((), (), s32[]{:S(2)}) async-start(), calls=%async_computation | async-start | bytes 2949120 | tf_op jit(solution)/shard_map/all_gather | solution.py:162
  12.0 0.7 copy-start.5
  13.5 0.9 copy-start.3
  13.5 1.0 %copy-start.4 = (s32[1,6]{1,0:T(1,128)S(1)}, s32[1,6]{1,0:T(1,128)}, u32[]{:S(2)}) copy-start(s32[1,6]{1,0:T(1,128)} %param.13) | copy-start | bytes 76
  18.7 0.9 copy-start.2
  26.3 4.6 %collective-permute-start.1 = (bf16[1,2,384,384]{2,3,1,0:T(8,128)(2,1)S(1)}, bf16[1,2,384,384]{2,3,1,0:T(8,128)(2,1)S(1)}, u32[]{:S(2)}, u32[]{:S(2)}) collective-permute-start(bf16[1,2,384,384]{2,3,1,0:T(8,128)(2,1)S(1)} %copy.58), channel_id=1, source_target_pairs={{4,0},{8,4},{12,8},{5,1},{9,5},{13,9},{6,2},{10,6},{14,10},{7,3},{... | collective-permute-start | bytes 1769480 | tf_op jit(solution)/shard_map/ppermute | solution.py:22
  27.6 4.7 %collective-permute-start = (bf16[1,2,384,384]{2,3,1,0:T(8,128)(2,1)S(1)}, bf16[1,2,384,384]{2,3,1,0:T(8,128)(2,1)S(1)}, u32[]{:S(2)}, u32[]{:S(2)}) collective-permute-start(bf16[1,2,384,384]{2,3,1,0:T(8,128)(2,1)S(1)} %copy.58), channel_id=1, source_target_pairs={{0,4},{4,8},{8,12},{1,5},{5,9},{9,13},{2,6},{6,10},{10,14},{3,7},{... | collective-permute-start | bytes 1769480 | tf_op jit(solution)/shard_map/ppermute | solution.py:20
Sparse Core Ops, SparseCore 0:
  26.5 52.7 all-gather.1
